TPU v7x, 512 devices: a whole 4x8x8 slice. The times are simulated.
512 devices in a mesh: row: 32 (over z_hi, x, core), col: 16 (over z_lo, y).
Axes of the slice: x: 4, y: 8, z: 8 (z_hi: 4, z_lo: 2; z = z_hi * 2 + z_lo), core: 2. Of those that a mesh axis runs over, the one named last changes fastest.
Arguments:
- embeddings: float32 [16384, 768], P(('row', 'col')), may hold values from -0.21650635 to 0.21650635
- sharpness: float32 [16384], P(('row', 'col')), may hold values from 0.5 to 4
- soft_labels: float32 [16384, 256], P(('row', 'col')), may hold values from 0 to 1
- seed_mask: int32 [16384], P(('row', 'col')), may hold values 0 or 1
- tile_mask: int32 [512, 512], P('row'), may hold values from 0 to 1, as said below
Outputs:
- spread_labels: float32 [16384, 256], P(('row', 'col'))
Inputs may be any that keep to these rules, and one draw needn't show every extreme that they name: Every diagonal entry tile_mask[p, p] is 1.
All inputs are finite; a program needn't handle non-finite values. No bound on the sum of `seed_mask` on one device may be relied on, other than what follows from the above.
Results may differ from a plain program's by a relative error of at most 0.0003.
Values sent between devices are 32-bit elements; how exact they have to be, the bound alone decides.
No kernel may reach another device: no remote copies, remote signals or barrier semaphores. Data moves between devices by JAX's collectives and lax.ppermute only.
A program may use at most 64 MiB of HBM per device.

v0:
```python
import jax
import jax.numpy as jnp
from jax import lax
from jax.sharding import PartitionSpec as P

ITERS = 3


def kernel_tile(row_emb, row_squares, row_width, col_emb, col_width, col_mask):
    cross = jnp.dot(
        row_emb, col_emb.T, precision=lax.Precision.HIGHEST, preferred_element_type=jnp.float32
    )
    col_squares = jnp.sum(col_emb * col_emb, axis=1)
    distance = row_squares[:, None] + col_squares[None, :] - 2.0 * cross
    return jnp.exp(-(distance * row_width[:, None] * col_width[None, :])) * col_mask


def local(embeddings, sharpness, soft_labels, seed_mask, tile_mask):
    n_row = lax.axis_size("row")
    n_col = lax.axis_size("col")
    col_index = lax.axis_index("col")
    piece = embeddings.shape[0]
    seeded = seed_mask.astype(jnp.float32)[:, None] * soft_labels
    row_emb, row_width = (
        lax.all_gather(embeddings, "col", axis=0, tiled=True),
        lax.all_gather(sharpness, "col", axis=0, tiled=True),
    )
    row_squares = jnp.sum(row_emb * row_emb, axis=1)
    block_rows = row_emb.shape[0]
    col_rows = piece * n_row
    grouped = tile_mask.reshape(n_col, n_row, n_col)
    chosen = lax.dynamic_index_in_dim(grouped, col_index, axis=2, keepdims=False)
    col_mask = jnp.broadcast_to(chosen[:, None, :, None], (n_col, piece, n_row, piece))
    col_mask = col_mask.reshape(block_rows, col_rows).astype(jnp.float32)
    col_emb, col_width = (
        lax.all_gather(embeddings, "row", axis=0, tiled=True),
        lax.all_gather(sharpness, "row", axis=0, tiled=True),
    )
    labels = seeded
    for iteration in range(ITERS):
        col_labels = lax.all_gather(labels, "row", axis=0, tiled=True)
        weights = kernel_tile(row_emb, row_squares, row_width, col_emb, col_width, col_mask)
        partial_value = jnp.dot(
            weights, col_labels, precision=lax.Precision.HIGHEST, preferred_element_type=jnp.float32
        )
        degree = jnp.sum(weights, axis=1)
        total_part, total_degree = lax.psum((partial_value, degree), "col")
        own_part = lax.dynamic_slice_in_dim(total_part, col_index * piece, piece, 0)
        own_degree = lax.dynamic_slice_in_dim(total_degree, col_index * piece, piece, 0)
        labels = 0.9 * own_part / own_degree[:, None] + 0.1 * seeded
    return labels


def solution(mesh):
    return jax.shard_map(
        local,
        mesh=mesh,
        in_specs=(
            P(("row", "col"), None),
            P(("row", "col")),
            P(("row", "col"), None),
            P(("row", "col")),
            P("row", None),
        ),
        out_specs=P(("row", "col"), None),
        check_vma=False,
    )
```

profile of v0, /device:TPU:2, one launch (start us, length us, event | category | flops | bytes accessed | tf_op | source)
XLA Modules:
  0.0 762.3 jit_solution(18345925877665009551)
XLA Ops:
  6.5 0.7 all-gather.6.cloned.1.call-update
  7.3 0.7 all-gather.8.cloned.1.call-update
  8.1 0.7 convert_element_type.16
  8.7 1.4 broadcast_multiply_fusion
  10.2 0.9 reshape.14
  11.1 0.3 convert_reduce_fusion
  11.4 4.4 broadcast_in_dim.2
  15.8 7.7 %convert_element_type.15 = f32[512,1024]{1,0:T(8,128)} reshape(f32[16,32,32,32]{3,2,1,0:T(8,128)} %broadcast_in_dim.2) | data formatting | bytes 4194304 | tf_op jit(solution)/shard_map/convert_element_type | solution.py:34
  23.5 1.3 dynamic-slice.1
  24.7 1.3 dynamic-slice
  27.4 0.2 dynamic-update-slice.1
  27.8 35.9 %all-reduce = f32[512]{0:T(512)S(1)} all-reduce(f32[512]{0:T(512)S(1)} %dynamic-update-slice), channel_id=1, replica_groups=mesh['row'=32,'col'=16] {'col'}, use_global_device_ids=true, to_apply=%add | all-reduce | flops 512 | bytes 4096
  63.7 68.1 %all-reduce.1 = f32[1024]{0:T(1024)S(1)} all-reduce(f32[1024]{0:T(1024)S(1)} %dynamic-update-slice.1), channel_id=1, replica_groups=mesh['row'=32,'col'=16] {'row'}, use_global_device_ids=true, to_apply=%add.1 | all-reduce | flops 1024 | bytes 8192
  131.8 1.6 multiply_reduce_fusion.1
  133.4 16.2 %all-gather.8.cloned.1.call-done = f32[1024,768]{1,0:T(8,128)} async-done(((f32[32,768]{1,0:T(8,128)}), f32[1024,768]{1,0:T(8,128)}) %all-gather.8.cloned.1.call-update) | async-done | bytes 3145744 | tf_op jit(solution)/shard_map/all_gather | solution.py:36
  149.6 2.3 multiply_reduce_fusion
  151.9 0.5 copy-done
  152.4 7.7 %fusion = (f32[512]{0:T(512)S(1)}, f32[512,1024]{1,0:T(8,128)S(1)}) fusion(f32[512,1024]{1,0:T(8,128)} %convert_element_type.15, f32[1024]{0:T(1024)S(1)} %all-reduce.1, f32[512]{0:T(512)S(1)} %all-reduce, f32[512,768]{1,0:T(8,128)} %all-gather.6.cloned.1.call-done, f32[1024,768]{1,0:T(8,128)S(1)} %copy-done, f32[1024]{0:T(1024)S(1)} %multiply_reduce_fusion, ...), kind=kOutput, calls=%fused_computation.8 | convolution fusion | flops 4836032000 | bytes 8927232 | tf_op jit(solution)/shard_map/dot_general | solution.py:10
  160.1 47.2 %all-gather.10.cloned.1.call-done = f32[1024,256]{1,0:T(8,128)} async-done(((f32[32,256]{1,0:T(8,128)}), f32[1024,256]{1,0:T(8,128)}) %all-gather.10.cloned.1.call-update) | async-done | bytes 1048592 | tf_op jit(solution)/shard_map/all_gather | solution.py:41
  207.3 3.8 fusion.1
  211.2 33.8 %psum.29 = f32[512]{0:T(512)S(1)} all-reduce(f32[512]{0:T(512)S(1)} %get-tuple-element.5), channel_id=1, replica_groups=mesh['row'=32,'col'=16] {'col'}, use_global_device_ids=true, to_apply=%region_4.5 | all-reduce | flops 512 | bytes 4096 | tf_op jit(solution)/shard_map/psum | solution.py:47
  245.1 106.3 %all-reduce.6.cloned.1.call-done = f32[512,256]{1,0:T(8,128)} async-done(((f32[512,256]{1,0:T(8,128)}), f32[512,256]{1,0:T(8,128)}) %all-reduce.6.cloned.1.call-update) | async-done | bytes 524304 | tf_op jit(solution)/shard_map/psum | solution.py:47
  351.3 1.5 divide_add_fusion.2
  352.8 0.2 all-reduce.8.cloned.1.call-start
  353.0 55.5 %all-gather.12.cloned.1.call-done = f32[1024,256]{1,0:T(8,128)} async-done(((f32[32,256]{1,0:T(8,128)}), f32[1024,256]{1,0:T(8,128)}) %all-gather.12.cloned.1.call-update) | async-done | bytes 1048592 | tf_op jit(solution)/shard_map/all_gather | solution.py:41
  408.6 3.8 fusion.2
  412.5 140.1 %all-reduce.8.cloned.1.call-done = f32[512,256]{1,0:T(8,128)} async-done(((f32[512,256]{1,0:T(8,128)}), f32[512,256]{1,0:T(8,128)}) %all-reduce.8.cloned.1.call-update) | async-done | bytes 524304 | tf_op jit(solution)/shard_map/psum | solution.py:47
  552.6 1.5 divide_add_fusion.1
  554.1 55.9 %all-gather.14.cloned.1.call-done = f32[1024,256]{1,0:T(8,128)} async-done(((f32[32,256]{1,0:T(8,128)}), f32[1024,256]{1,0:T(8,128)}) %all-gather.14.cloned.1.call-update) | async-done | bytes 1048592 | tf_op jit(solution)/shard_map/all_gather | solution.py:41
  610.0 3.8 fusion.3
  613.9 140.1 %all-reduce.10.cloned.1.call-done = f32[512,256]{1,0:T(8,128)} async-done(((f32[512,256]{1,0:T(8,128)}), f32[512,256]{1,0:T(8,128)}) %all-reduce.10.cloned.1.call-update) | async-done | bytes 524304 | tf_op jit(solution)/shard_map/psum | solution.py:47
  754.0 1.5 divide_add_fusion
  (23 shorter events, 0.6 us)
Async XLA Ops:
  6.5 125.3 %all-gather.6.cloned.1.call-start = ((), (), s32[]{:S(2)}) async-start(), calls=%async_computation | async-start | bytes 1671168 | tf_op jit(solution)/shard_map/all_gather | solution.py:25
  7.3 142.4 %all-gather.8.cloned.1.call-start = ((), (), s32[]{:S(2)}) async-start(), calls=%async_computation.1 | async-start | bytes 3244032 | tf_op jit(solution)/shard_map/all_gather | solution.py:36
  8.0 199.3 %all-gather.10.cloned.1.call-start = ((), (), s32[]{:S(2)}) async-start(), calls=%async_computation.2 | async-start | bytes 1081344 | tf_op jit(solution)/shard_map/all_gather | solution.py:41
  10.2 341.2 %all-reduce.6.cloned.1.call-start = ((), (), s32[]{:S(2)}) async-start(), calls=%async_computation.3 | async-start | bytes 1048576 | tf_op jit(solution)/shard_map/psum | solution.py:47
  15.8 11.6 %copy-start.2 = (f32[32]{0:T(128)S(1)}, f32[32]{0:T(128)}, u32[]{:S(2)}) copy-start(f32[32]{0:T(128)} %param.6) | copy-start | bytes 388
  149.6 2.8 copy-start
  207.3 144.0 %copy-start.1 = (f32[32,256]{1,0:T(8,128)S(1)}, f32[32,256]{1,0:T(8,128)}, u32[]{:S(2)}) copy-start(f32[32,256]{1,0:T(8,128)} %param.7) | copy-start | bytes 98308
  211.2 197.4 %all-gather.12.cloned.1.call-start = ((), (), s32[]{:S(2)}) async-start(), calls=%async_computation.4 | async-start | bytes 1081344 | tf_op jit(solution)/shard_map/all_gather | solution.py:41
  352.8 199.8 %all-reduce.8.cloned.1.call-start = ((), (), s32[]{:S(2)}) async-start(), calls=%async_computation.5 | async-start | bytes 1048576 | tf_op jit(solution)/shard_map/psum | solution.py:47
  412.5 197.5 %all-gather.14.cloned.1.call-start = ((), (), s32[]{:S(2)}) async-start(), calls=%async_computation.6 | async-start | bytes 1081344 | tf_op jit(solution)/shard_map/all_gather | solution.py:41
  554.1 199.9 %all-reduce.10.cloned.1.call-start = ((), (), s32[]{:S(2)}) async-start(), calls=%async_computation.7 | async-start | bytes 1048576 | tf_op jit(solution)/shard_map/psum | solution.py:47
Sparse Core Ops, SparseCore 0:
  9.4 77.4 all-gather.5
  90.0 59.5 all-gather.7
  152.8 54.5 all-gather.9
  211.3 140.0 all-reduce.5
  354.3 54.2 all-gather.11
  412.6 139.9 all-reduce.7
  555.7 54.2 all-gather.13
  614.0 139.9 all-reduce.9
where the time goes:
time: 763 us; the launch traced here: 762 us
  waiting for transfers between devices  563 us (74%)
  blocking collectives  138 us (18%)
  matrix products  19.2 us (3%)
  local copies, waits for them, and re-layouts  16.6 us (2%)
  between operations  14.8 us (2%)
  other arithmetic  10.6 us (1%)
    psum x3, waiting for transfers between devices, local(): total_part, total_degree = lax.psum((partial_value, degree), 'col')  387 us
    all_gather x3, waiting for transfers between devices, local(): col_labels = lax.all_gather(labels, 'row', axis=0, tiled=True)  159 us
    unnamed x2, blocking collectives  104 us
    psum x1, blocking collectives, local(): total_part, total_degree = lax.psum((partial_value, degree), 'col')  33.8 us
    all_gather x1, waiting for transfers between devices, local(): lax.all_gather(embeddings, 'row', axis=0, tiled=True)  16.2 us
  transfers between devices with their start and end apart: 8, of which 7 were waited for; matrix products, arithmetic and copies ran while one was open for 4% of the time, Pallas kernels for 0%

commit v1 on v0

--- a/solution.py
+++ b/solution.py
@@ -4,6 +4,14 @@
 from jax.sharding import PartitionSpec as P
 
 ITERS = 3
+
+
+def touch_cells(frame, on_dim):
+    fresh = jnp.concatenate(
+        lax.all_to_all(jnp.stack([frame for _ in range(lax.axis_size("row"))]), "row", 0, 0),
+        axis=on_dim,
+    )
+    return fresh
 
 
 def kernel_tile(row_emb, row_squares, row_width, col_emb, col_width, col_mask):
@@ -38,7 +46,7 @@
     )
     labels = seeded
     for iteration in range(ITERS):
-        col_labels = lax.all_gather(labels, "row", axis=0, tiled=True)
+        col_labels = touch_cells(labels, 0)
         weights = kernel_tile(row_emb, row_squares, row_width, col_emb, col_width, col_mask)
         partial_value = jnp.dot(
             weights, col_labels, precision=lax.Precision.HIGHEST, preferred_element_type=jnp.float32

time: 763 us -> 666 us (0.87)
  waiting for transfers between devices: 563 us -> 396 us
  blocking collectives: 138 us -> 200 us
  starting transfers between devices: 0.47 us -> 13.6 us
    all_gather x3 -> x0, waiting for transfers between devices: 159 us -> none  [local(): col_labels = lax.all_gather(labels, 'row', axis=0, tiled=True)]
    all_to_all x0 -> x2, blocking collectives: none -> 66.4 us  [touch_cells(): lax.all_to_all(jnp.stack([frame for _ in range(lax.axis_size('row'))]), '...]
    all_to_all x0 -> x1, starting transfers between devices: none -> 13.5 us  [touch_cells(): lax.all_to_all(jnp.stack([frame for _ in range(lax.axis_size('row'))]), '...]
  transfers between devices with their start and end apart: 8 -> 6, of which waited for: 7 -> 4; matrix products, arithmetic and copies ran while one was open for 4% -> 4% of each run, Pallas kernels for 0% -> 0%
where the time goes in v1:
time: 666 us; the launch traced here: 665 us
  waiting for transfers between devices  396 us (59%)
  blocking collectives  200 us (30%)
  local copies, waits for them, and re-layouts  17.3 us (3%)
  matrix products  15.6 us (2%)
  between operations  14.6 us (2%)
  starting transfers between devices  13.6 us (2%)
  other arithmetic  8.78 us (1%)
    psum x3, waiting for transfers between devices, local(): total_part, total_degree = lax.psum((partial_value, degree), 'col')  385 us
    unnamed x2, blocking collectives  99.2 us
    all_to_all x2, blocking collectives, touch_cells(): lax.all_to_all(jnp.stack([frame for _ in range(lax.axis_size('row'))]), '...  66.4 us
    psum x1, blocking collectives, local(): total_part, total_degree = lax.psum((partial_value, degree), 'col')  34.2 us
    all_to_all x1, starting transfers between devices, touch_cells(): lax.all_to_all(jnp.stack([frame for _ in range(lax.axis_size('row'))]), '...  13.5 us
  transfers between devices with their start and end apart: 6, of which 4 were waited for; matrix products, arithmetic and copies ran while one was open for 4% of the time, Pallas kernels for 0%

profile of v1, /device:TPU:2, one launch (start us, length us, event | category | flops | bytes accessed | tf_op | source)
XLA Modules:
  0.0 665.3 jit_solution(10481367444419149309)
XLA Ops:
  6.5 0.7 all-gather.3.cloned.1.call-update
  7.3 0.7 all-gather.5.cloned.1.call-update
  8.0 0.7 convert_element_type.16
  8.7 0.8 broadcast_multiply_fusion
  9.5 1.1 stack.6
  10.6 13.5 %all-to-all-start = ((f32[32,32,256]{2,1,0:T(8,128)}), f32[32,32,256]{2,1,0:T(8,128)S(1)}, u32[]{:S(2)}, u32[]{:S(2)}) async-start(f32[32,32,256]{2,1,0:T(8,128)} %stack.6), calls=%async_computation | async-start | bytes 2097152 | tf_op jit(solution)/shard_map/all_to_all | solution.py:11
  24.3 0.3 convert_reduce_fusion
  24.6 4.4 broadcast_in_dim.2
  28.9 7.8 %convert_element_type.15 = f32[512,1024]{1,0:T(8,128)} reshape(f32[16,32,32,32]{3,2,1,0:T(8,128)} %broadcast_in_dim.2) | data formatting | bytes 4194304 | tf_op jit(solution)/shard_map/convert_element_type | solution.py:42
  36.7 1.3 dynamic-slice.1
  37.9 1.3 dynamic-slice
  40.6 0.2 dynamic-update-slice.1
  40.9 0.2 dynamic-update-slice
  41.1 35.1 %all-reduce = f32[512]{0:T(512)S(1)} all-reduce(f32[512]{0:T(512)S(1)} %dynamic-update-slice), channel_id=1, replica_groups=mesh['row'=32,'col'=16] {'col'}, use_global_device_ids=true, to_apply=%add | all-reduce | flops 512 | bytes 4096
  76.2 64.1 %all-reduce.1 = f32[1024]{0:T(1024)S(1)} all-reduce(f32[1024]{0:T(1024)S(1)} %dynamic-update-slice.1), channel_id=1, replica_groups=mesh['row'=32,'col'=16] {'row'}, use_global_device_ids=true, to_apply=%add.1 | all-reduce | flops 1024 | bytes 8192
  140.3 1.6 multiply_reduce_fusion.1
  141.9 8.7 %all-gather.5.cloned.1.call-done = f32[1024,768]{1,0:T(8,128)} async-done(((f32[32,768]{1,0:T(8,128)}), f32[1024,768]{1,0:T(8,128)}) %all-gather.5.cloned.1.call-update) | async-done | bytes 3145744 | tf_op jit(solution)/shard_map/all_gather | solution.py:44
  150.6 2.3 multiply_reduce_fusion
  152.9 0.5 copy-done
  153.4 7.7 %fusion = (f32[512]{0:T(512)S(1)}, f32[512,1024]{1,0:T(8,128)S(1)}) fusion(f32[512,1024]{1,0:T(8,128)} %convert_element_type.15, f32[1024]{0:T(1024)S(1)} %all-reduce.1, f32[512]{0:T(512)S(1)} %all-reduce, f32[512,768]{1,0:T(8,128)} %all-gather.3.cloned.1.call-done, f32[1024,768]{1,0:T(8,128)S(1)} %copy-done, f32[1024]{0:T(1024)S(1)} %multiply_reduce_fusion, ...), kind=kOutput, calls=%fused_computation.8 | convolution fusion | flops 4836032000 | bytes 8927232 | tf_op jit(solution)/shard_map/dot_general | solution.py:18
  161.2 2.6 fusion.1
  163.9 34.2 %psum.29 = f32[512]{0:T(512)S(1)} all-reduce(f32[512]{0:T(512)S(1)} %get-tuple-element.5), channel_id=1, replica_groups=mesh['row'=32,'col'=16] {'col'}, use_global_device_ids=true, to_apply=%region_4.5 | all-reduce | flops 512 | bytes 4096 | tf_op jit(solution)/shard_map/psum | solution.py:55
  198.2 105.2 %all-reduce.6.cloned.1.call-done = f32[512,256]{1,0:T(8,128)} async-done(((f32[512,256]{1,0:T(8,128)}), f32[512,256]{1,0:T(8,128)}) %all-reduce.6.cloned.1.call-update) | async-done | bytes 524304 | tf_op jit(solution)/shard_map/psum | solution.py:55
  303.3 0.8 divide_add_fusion.2
  304.3 33.2 %all_to_all.15 = f32[32,32,256]{2,1,0:T(8,128)S(1)} all-to-all(f32[32,32,256]{2,1,0:T(8,128)S(1)} %stack.7), channel_id=1, replica_groups=mesh['row'=32,'col'=16] {'row'}, dimensions={0} | all-to-all | bytes 2097152 | tf_op jit(solution)/shard_map/all_to_all | solution.py:11
  337.5 2.6 fusion.2
  340.2 140.1 %all-reduce.8.cloned.1.call-done = f32[512,256]{1,0:T(8,128)} async-done(((f32[512,256]{1,0:T(8,128)}), f32[512,256]{1,0:T(8,128)}) %all-reduce.8.cloned.1.call-update) | async-done | bytes 524304 | tf_op jit(solution)/shard_map/psum | solution.py:55
  480.3 0.8 divide_add_fusion.1
  481.3 33.2 %all_to_all.16 = f32[32,32,256]{2,1,0:T(8,128)S(1)} all-to-all(f32[32,32,256]{2,1,0:T(8,128)S(1)} %stack.8), channel_id=1, replica_groups=mesh['row'=32,'col'=16] {'row'}, dimensions={0} | all-to-all | bytes 2097152 | tf_op jit(solution)/shard_map/all_to_all | solution.py:11
  514.5 2.6 fusion.3
  517.1 140.2 %all-reduce.10.cloned.1.call-done = f32[512,256]{1,0:T(8,128)} async-done(((f32[512,256]{1,0:T(8,128)}), f32[512,256]{1,0:T(8,128)}) %all-reduce.10.cloned.1.call-update) | async-done | bytes 524304 | tf_op jit(solution)/shard_map/psum | solution.py:55
  657.3 1.5 divide_add_fusion
  (23 shorter events, 0.7 us)
Async XLA Ops:
  6.5 17.6 %copy-start.2 = (s32[16,512]{1,0:T(8,128)S(1)}, s32[16,512]{1,0:T(8,128)}, u32[]{:S(2)}) copy-start(s32[16,512]{1,0:T(8,128)} %param.9) | copy-start | bytes 98308
  6.5 133.7 %all-gather.3.cloned.1.call-start = ((), (), s32[]{:S(2)}) async-start(), calls=%async_computation.3 | async-start | bytes 1671168 | tf_op jit(solution)/shard_map/all_gather | solution.py:33
  7.3 143.3 %all-gather.5.cloned.1.call-start = ((), (), s32[]{:S(2)}) async-start(), calls=%async_computation.4 | async-start | bytes 3244032 | tf_op jit(solution)/shard_map/all_gather | solution.py:44
  10.6 150.5 %all-to-all-start = ((f32[32,32,256]{2,1,0:T(8,128)}), f32[32,32,256]{2,1,0:T(8,128)S(1)}, u32[]{:S(2)}, u32[]{:S(2)}) async-start(f32[32,32,256]{2,1,0:T(8,128)} %stack.6), calls=%async_computation | async-start | bytes 2097152 | tf_op jit(solution)/shard_map/all_to_all | solution.py:11
  24.1 279.2 %all-reduce.6.cloned.1.call-start = ((), (), s32[]{:S(2)}) async-start(), calls=%async_computation.5 | async-start | bytes 1048576 | tf_op jit(solution)/shard_map/psum | solution.py:55
  28.9 11.7 %copy-start.3 = (f32[32]{0:T(128)S(1)}, f32[32]{0:T(128)}, u32[]{:S(2)}) copy-start(f32[32]{0:T(128)} %param.6) | copy-start | bytes 388
  150.6 2.8 copy-start
  161.1 142.2 %copy-start.1 = (f32[32,256]{1,0:T(8,128)S(1)}, f32[32,256]{1,0:T(8,128)}, u32[]{:S(2)}) copy-start(f32[32,256]{1,0:T(8,128)} %param.7) | copy-start | bytes 98308
  163.8 316.5 %all-reduce.8.cloned.1.call-start = ((), (), s32[]{:S(2)}) async-start(), calls=%async_computation.6 | async-start | bytes 1048576 | tf_op jit(solution)/shard_map/psum | solution.py:55
  340.1 317.2 %all-reduce.10.cloned.1.call-start = ((), (), s32[]{:S(2)}) async-start(), calls=%async_computation.7 | async-start | bytes 1048576 | tf_op jit(solution)/shard_map/psum | solution.py:55
Sparse Core Ops, SparseCore 0:
  9.4 78.8 all-gather.2
  91.4 59.1 all-gather.4
  163.9 139.3 all-reduce.5
  340.3 140.0 all-reduce.7
  517.3 139.9 all-reduce.9
